TPU v7x, 1024 devices: a whole 4x4x32 slice. The times are simulated.
1024 devices in a mesh: tm: 16 (over x, y), dp: 64 (over z, core).
Axes of the slice: x: 4, y: 4, z: 32, core: 2. Of those that a mesh axis runs over, the one named last changes fastest.
Arguments:
- video: bfloat16 [64, 16, 8, 24, 128], P('dp', 'tm'), may hold values from -17 to 17
- cotangent: bfloat16 [64, 16, 8, 24, 128], P('dp', 'tm'), may hold values from -6 to 6
- conv1_weight: bfloat16 [3456, 128], replicated, may hold values from -0.109375 to 0.109375
- conv2_weight: bfloat16 [3456, 128], replicated, may hold values from -0.109375 to 0.109375
Outputs:
- block_out: bfloat16 [64, 16, 8, 24, 128], P('dp', 'tm')
- grad_video: float32 [64, 16, 8, 24, 128], P('dp', 'tm')
- grad_conv1: float32 [3456, 128], P('dp', 'tm')
- grad_conv2: float32 [3456, 128], P('dp', 'tm')
All inputs are finite; a program needn't handle non-finite values.
Results may differ from a plain program's by a relative error of at most 0.022.
Values may be sent and summed in bfloat16 or wider, within the bound.
No kernel may reach another device: no remote copies, remote signals or barrier semaphores. Data moves between devices by JAX's collectives and lax.ppermute only.
A program may use at most 64 MiB of HBM per device.

v0:
```python
import math

import jax
import jax.numpy as jnp
from jax import lax
from jax.sharding import PartitionSpec as P

GROUPS = 32


EPSILON = 1e-06


def from_behind(block, axis, distance):
    devices = range(lax.axis_size(axis))
    route = [(i - distance, i) for i in devices if i - distance in devices]
    return lax.ppermute(block, axis, route)


def group_sums(totals):
    return lax.psum(totals, "tm")


def normalize(values, members):
    grouped = values.reshape(-1, GROUPS, values.shape[-1] // GROUPS)
    (summed,) = group_sums((jnp.sum(grouped, axis=(0, 2)),))
    average = summed / members
    centered = grouped - average[None, :, None]
    (squares,) = group_sums((jnp.sum(centered * centered, axis=(0, 2)),))
    variance = squares / members
    inv_scale = lax.rsqrt(variance + EPSILON)
    return (centered * inv_scale[None, :, None], inv_scale)


def norm_backward(grad_act, normed, inv_scale, members):
    logistic = jax.nn.sigmoid(normed)
    grad_normed = grad_act * logistic * (1.0 + normed * (1.0 - logistic))
    first_sum, second_sum = group_sums(
        (jnp.sum(grad_normed, axis=(0, 2)), jnp.sum(grad_normed * normed, axis=(0, 2)))
    )
    first_mean = first_sum / members
    second_mean = second_sum / members
    return inv_scale[None, :, None] * (
        grad_normed - first_mean[None, :, None] - normed * second_mean[None, :, None]
    )


def earlier_frames(own_frame):
    stacked = [own_frame]
    for offset in (1, 2):
        stacked.insert(0, from_behind(own_frame, "tm", offset))
    return jnp.concatenate(stacked, axis=0)


def later_frames(own_frame):
    stacked = [own_frame]
    for offset in (1, 2):
        stacked.append(from_behind(own_frame, "tm", -offset))
    return jnp.concatenate(stacked, axis=0)


def forward_patches(stacked):
    frames = stacked.shape[0] - 2
    height, width, chans = (stacked.shape[1], stacked.shape[2], stacked.shape[3])
    padded = jnp.pad(stacked, ((0, 0), (1, 1), (1, 1), (0, 0)))
    columns = [
        padded[tap_t : tap_t + frames, tap_h : tap_h + height, tap_w : tap_w + width, :]
        for tap_t in range(3)
        for tap_h in range(3)
        for tap_w in range(3)
    ]
    return jnp.concatenate(columns, axis=-1).reshape(frames * height * width, 27 * chans)


def backward_patches(stacked):
    frames = stacked.shape[0] - 2
    height, width, chans = (stacked.shape[1], stacked.shape[2], stacked.shape[3])
    padded = jnp.pad(stacked, ((0, 0), (1, 1), (1, 1), (0, 0)))
    columns = [
        padded[
            2 - tap_t : 2 - tap_t + frames,
            2 - tap_h : 2 - tap_h + height,
            2 - tap_w : 2 - tap_w + width,
            :,
        ]
        for tap_t in range(3)
        for tap_h in range(3)
        for tap_w in range(3)
    ]
    return jnp.concatenate(columns, axis=-1).reshape(frames * height * width, 27 * chans)


def flipped(weight):
    chans = weight.shape[1]
    return weight.reshape(27, chans, chans).transpose(0, 2, 1).reshape(27 * chans, chans)


def weight_grad(patches, grads):
    return lax.dot_general(
        patches, grads, (((0,), (0,)), ((), ())), preferred_element_type=jnp.float32
    )


def reduce_grads(grads):
    split_part = (
        lax.psum_scatter(grads[0], "dp", scatter_dimension=0, tiled=True),
        lax.psum_scatter(grads[1], "dp", scatter_dimension=0, tiled=True),
    )
    return (
        lax.psum_scatter(
            split_part[0].astype(jnp.bfloat16), "tm", scatter_dimension=1, tiled=True
        ).astype(jnp.float32),
        lax.psum_scatter(
            split_part[1].astype(jnp.bfloat16), "tm", scatter_dimension=1, tiled=True
        ).astype(jnp.float32),
    )


def body(video, cotangent, conv1_weight, conv2_weight):
    own_frame = video[0]
    grad_out = cotangent[0]
    layout = own_frame.shape
    height, width, chans = (layout[1], layout[2], layout[3])
    members = float(lax.axis_size("tm") * height * width * (chans // GROUPS))
    grouping = (-1, GROUPS, chans // GROUPS)
    first_normed, first_scale = normalize(own_frame.astype(jnp.float32), members)
    first_act = (first_normed * jax.nn.sigmoid(first_normed)).astype(jnp.bfloat16).reshape(layout)
    first_patches = forward_patches(earlier_frames(first_act))
    hidden = (
        jnp.dot(first_patches, conv1_weight, preferred_element_type=jnp.float32)
        .astype(jnp.bfloat16)
        .reshape(layout)
    )
    second_normed, second_scale = normalize(hidden.astype(jnp.float32), members)
    second_act = (
        (second_normed * jax.nn.sigmoid(second_normed)).astype(jnp.bfloat16).reshape(layout)
    )
    second_patches = forward_patches(earlier_frames(second_act))
    mixed = jnp.dot(second_patches, conv2_weight, preferred_element_type=jnp.float32).reshape(
        layout
    )
    block_out = (own_frame.astype(jnp.float32) + mixed).astype(jnp.bfloat16)
    grad_w2 = weight_grad(second_patches, grad_out.reshape(-1, chans))
    grad_second = jnp.dot(
        backward_patches(later_frames(grad_out)),
        flipped(conv2_weight),
        preferred_element_type=jnp.float32,
    )
    grad_hidden = norm_backward(grad_second.reshape(grouping), second_normed, second_scale, members)
    grad_hidden = grad_hidden.astype(jnp.bfloat16).reshape(layout)
    grad_w1 = weight_grad(first_patches, grad_hidden.reshape(-1, chans))
    grad_first = jnp.dot(
        backward_patches(later_frames(grad_hidden)),
        flipped(conv1_weight),
        preferred_element_type=jnp.float32,
    )
    grad_video = grad_out.astype(jnp.float32) + norm_backward(
        grad_first.reshape(grouping), first_normed, first_scale, members
    ).reshape(layout)
    total_w1, total_w2 = reduce_grads((grad_w1, grad_w2))
    factor = 1.0 / math.sqrt(lax.axis_size("tm") * lax.axis_size("dp") * height * width)
    return (block_out[None], grad_video[None], total_w1 * factor, total_w2 * factor)


def solution(mesh):
    placed = (P("dp", "tm", None, None, None), P("dp", "tm", None, None, None), P(), P())
    return jax.shard_map(
        body,
        mesh=mesh,
        in_specs=placed,
        out_specs=(
            P("dp", "tm", None, None, None),
            P("dp", "tm", None, None, None),
            P("dp", "tm"),
            P("dp", "tm"),
        ),
        check_vma=False,
    )
```

profile of v0, /device:TPU:32, one launch (start us, length us, event | category | flops | bytes accessed | tf_op | source)
XLA Modules:
  0.0 605.9 jit_solution(3097729039031770766)
XLA Ops:
  1.8 40.7 %psum.56 = f32[32]{0:T(128)S(1)} all-reduce(f32[32]{0:T(128)S(1)} %reduce_sum.83), channel_id=1, replica_groups=mesh['tm'=16,'dp'=64] {'tm'}, use_global_device_ids=true, to_apply=%region_2.0 | all-reduce | flops 32 | bytes 256 | tf_op jit(solution)/shard_map/psum | solution.py:21
  44.3 35.5 %psum.57 = f32[32]{0:T(128)S(1)} all-reduce(f32[32]{0:T(128)S(1)} %reduce_sum.105), channel_id=1, replica_groups=mesh['tm'=16,'dp'=64] {'tm'}, use_global_device_ids=true, to_apply=%region_5.6 | all-reduce | flops 32 | bytes 256 | tf_op jit(solution)/shard_map/psum | solution.py:21
  80.5 1.5 fusion.59
  81.9 3.9 collective-permute-start.1
  85.9 1.9 collective-permute-start
  87.8 1.3 collective-permute-start.5
  89.0 1.3 collective-permute-start.4
  94.5 1.3 copy.99
  98.1 1.3 copy.112
  101.5 1.3 dynamic-slice.2
  110.3 42.3 %psum.58 = f32[32]{0:T(128)S(1)} all-reduce(f32[32]{0:T(128)S(1)} %reduce_sum.108), channel_id=1, replica_groups=mesh['tm'=16,'dp'=64] {'tm'}, use_global_device_ids=true, to_apply=%region_8.9 | all-reduce | flops 32 | bytes 256 | tf_op jit(solution)/shard_map/psum | solution.py:21
  153.1 35.5 %psum.59 = f32[32]{0:T(128)S(1)} all-reduce(f32[32]{0:T(128)S(1)} %reduce_sum.111), channel_id=1, replica_groups=mesh['tm'=16,'dp'=64] {'tm'}, use_global_device_ids=true, to_apply=%region_11.12 | all-reduce | flops 32 | bytes 256 | tf_op jit(solution)/shard_map/psum | solution.py:21
  189.4 4.5 collective-permute-start.3
  193.9 1.9 collective-permute-start.2
  200.6 35.5 %all-reduce.11 = (f32[32]{0:T(128)S(1)}, f32[32]{0:T(128)S(1)}) all-reduce(f32[32]{0:T(128)S(1)} %get-tuple-element.23, f32[32]{0:T(128)S(1)} %get-tuple-element.22), channel_id=1, replica_groups=mesh['tm'=16,'dp'=64] {'tm'}, use_global_device_ids=true, to_apply=%region_15.16 | all-reduce | flops 64 | bytes 512 | tf_op jit(solution)/shard_map/psum | solution.py:21
  239.1 1.3 collective-permute-start.6
  240.4 1.5 fusion.76
  244.0 3.9 collective-permute-done.7
  256.3 2.0 fusion.77
  258.3 122.9 %fusion.64 = (f32[64,128]{1,0:T(8,128)S(1)}, f32[64,128]{1,0:T(8,128)S(1)}) fusion(f32[3456,128]{1,0:T(8,128)S(1)} %fusion.76, f32[3456,128]{1,0:T(8,128)} %fusion.77), kind=kCustom, calls=%all-reduce-scatter.2 | all-reduce-scatter fusion | flops 1048577 | bytes 3608576
  381.2 1.9 collective-permute-start.19
  383.1 1.3 collective-permute-start.20
  384.4 1.3 collective-permute-start.21
  385.7 6.8 %collective-permute-start.22 = (bf16[64,128]{1,0:T(8,128)(2,1)S(1)}, bf16[64,128]{1,0:T(8,128)(2,1)S(1)}, u32[]{:S(2)}, u32[]{:S(2)}) collective-permute-start(bf16[64,128]{1,0:T(8,128)(2,1)S(1)} %convert.42), channel_id=1, source_target_pairs={{0,5},{1,6},{2,7},{3,8},{4,9},{5,10},{6,11},{7,12},{8,13},{9,14},{... | collective-permute-start | bytes 49160
  400.4 39.2 %all-reduce.10 = (f32[32]{0:T(128)S(1)}, f32[32]{0:T(128)S(1)}) all-reduce(f32[32]{0:T(128)S(1)} %get-tuple-element.21, f32[32]{0:T(128)S(1)} %get-tuple-element.20), channel_id=1, replica_groups=mesh['tm'=16,'dp'=64] {'tm'}, use_global_device_ids=true, to_apply=%region_19.20 | all-reduce | flops 64 | bytes 512 | tf_op jit(solution)/shard_map/psum | solution.py:21
  441.4 1.4 constant_dynamic-update-slice_fusion.49
  448.0 1.4 constant_dynamic-update-slice_fusion.40
  456.5 7.9 %collective-permute-start.27 = (bf16[54,128]{1,0:T(8,128)(2,1)S(1)}, bf16[54,128]{1,0:T(8,128)(2,1)S(1)}, u32[]{:S(2)}, u32[]{:S(2)}) collective-permute-start(bf16[54,128]{1,0:T(8,128)(2,1)S(1)} %slice.505), channel_id=1, source_target_pairs={{0,10},{1,11},{2,12},{3,13},{4,14},{5,15},{6,16},{7,17},{8,18},{9,... | collective-permute-start | bytes 41480
  465.8 10.3 %collective-permute-start.23 = (bf16[64,128]{1,0:T(8,128)(2,1)S(1)}, bf16[64,128]{1,0:T(8,128)(2,1)S(1)}, u32[]{:S(2)}, u32[]{:S(2)}) collective-permute-start(bf16[64,128]{1,0:T(8,128)(2,1)S(1)} %convert.42), channel_id=1, source_target_pairs={{0,6},{1,7},{2,8},{3,9},{4,10},{5,11},{6,12},{7,13},{8,14},{9,15},... | collective-permute-start | bytes 49160
  476.2 1.3 collective-permute-start.24
  477.5 6.2 %collective-permute-start.25 = (bf16[64,128]{1,0:T(8,128)(2,1)S(1)}, bf16[64,128]{1,0:T(8,128)(2,1)S(1)}, u32[]{:S(2)}, u32[]{:S(2)}) collective-permute-start(bf16[64,128]{1,0:T(8,128)(2,1)S(1)} %convert.42), channel_id=1, source_target_pairs={{0,8},{1,9},{2,10},{3,11},{4,12},{5,13},{6,14},{7,15},{8,16},{9,17... | collective-permute-start | bytes 49160
  483.7 8.1 %collective-permute-start.26 = (bf16[64,128]{1,0:T(8,128)(2,1)S(1)}, bf16[64,128]{1,0:T(8,128)(2,1)S(1)}, u32[]{:S(2)}, u32[]{:S(2)}) collective-permute-start(bf16[64,128]{1,0:T(8,128)(2,1)S(1)} %convert.42), channel_id=1, source_target_pairs={{0,9},{1,10},{2,11},{3,12},{4,13},{5,14},{6,15},{7,16},{8,17},{9,1... | collective-permute-start | bytes 49160
  491.8 1.9 collective-permute-start.18
  494.4 3.9 collective-permute-start.9
  498.3 2.2 collective-permute-start.10
  500.5 4.6 collective-permute-start.11
  505.1 1.6 collective-permute-start.12
  506.8 3.2 collective-permute-start.17
  510.0 2.5 fusion.27
  513.4 1.7 concatenate.358
  515.1 2.6 collective-permute-start.13
  517.7 3.5 collective-permute-start.14
  521.2 5.0 collective-permute-start.15
  526.2 1.8 collective-permute-start.16
  528.0 1.9 collective-permute-start.8
  530.0 3.1 collective-permute-done.8
  533.1 1.7 concatenate.357
  534.8 69.6 %all-reduce.12 = (bf16[54,128]{1,0:T(8,128)(2,1)S(1)}, bf16[54,128]{1,0:T(8,128)(2,1)S(1)}) all-reduce(bf16[54,128]{1,0:T(8,128)(2,1)S(1)} %dynamic-slice_convert_fusion.1, bf16[54,128]{1,0:T(8,128)(2,1)S(1)} %dynamic-slice_convert_fusion), channel_id=3, replica_groups=mesh['tm'=16,'dp'=64] {'tm'}, use_global_device_ids=true, to_apply=%region_21.22.clone | all-reduce | flops 13824 | bytes 55296
  (301 shorter events, 63.3 us)
Async XLA Ops:
  0.6 93.9 %copy-start.1 = (bf16[3456,128]{1,0:T(8,128)(2,1)S(1)}, bf16[3456,128]{1,0:T(8,128)(2,1)}, u32[]{:S(2)}) copy-start(bf16[3456,128]{1,0:T(8,128)(2,1)} %param.7) | copy-start | bytes 2654212
  43.2 47.1 %copy-start.26 = (f32[128]{0:T(128)}, f32[128]{0:T(128)S(1)}, u32[]{:S(2)}) copy-start(f32[128]{0:T(128)S(1)} %sub.91) | copy-start | bytes 1540
  80.5 9.9 %copy-start.28 = (f32[128]{0:T(128)}, f32[128]{0:T(128)S(1)}, u32[]{:S(2)}) copy-start(f32[128]{0:T(128)S(1)} %mul.150) | copy-start | bytes 1540
  81.9 22.1 %collective-permute-start.1 = (bf16[1,8,24,128]{3,2,1,0:T(8,128)(2,1)}, bf16[1,8,24,128]{3,2,1,0:T(8,128)(2,1)S(1)}, u32[]{:S(2)}, u32[]{:S(2)}) collective-permute-start(bf16[1,8,24,128]{3,2,1,0:T(8,128)(2,1)} %fusion.59), channel_id=1, source_target_pairs={{0,64},{64,128},{128,192},{192,256},{256,320},{320,384},{384,448},... | collective-permute-start | bytes 147464 | tf_op jit(solution)/shard_map/ppermute | solution.py:17
  85.9 18.2 %collective-permute-start = (bf16[1,8,24,128]{3,2,1,0:T(8,128)(2,1)}, bf16[1,8,24,128]{3,2,1,0:T(8,128)(2,1)}, u32[]{:S(2)}, u32[]{:S(2)}) collective-permute-start(bf16[1,8,24,128]{3,2,1,0:T(8,128)(2,1)} %fusion.59), channel_id=1, source_target_pairs={{0,128},{64,192},{128,256},{192,320},{256,384},{320,448},{384,512}... | collective-permute-start | bytes 147464 | tf_op jit(solution)/shard_map/ppermute | solution.py:17
  87.8 17.4 %collective-permute-start.5 = (bf16[1,8,24,128]{3,2,1,0:T(8,128)(2,1)}, bf16[1,8,24,128]{3,2,1,0:T(8,128)(2,1)S(1)}, u32[]{:S(2)}, u32[]{:S(2)}) collective-permute-start(bf16[1,8,24,128]{3,2,1,0:T(8,128)(2,1)} %bitcast.224), channel_id=1, source_target_pairs={{128,0},{192,64},{256,128},{320,192},{384,256},{448,320},{512,384}... | collective-permute-start | bytes 147464 | tf_op jit(solution)/shard_map/ppermute | solution.py:17
  89.0 16.2 %collective-permute-start.4 = (bf16[1,8,24,128]{3,2,1,0:T(8,128)(2,1)}, bf16[1,8,24,128]{3,2,1,0:T(8,128)(2,1)S(1)}, u32[]{:S(2)}, u32[]{:S(2)}) collective-permute-start(bf16[1,8,24,128]{3,2,1,0:T(8,128)(2,1)} %bitcast.225), channel_id=1, source_target_pairs={{64,0},{128,64},{192,128},{256,192},{320,256},{384,320},{448,384},... | collective-permute-start | bytes 147464 | tf_op jit(solution)/shard_map/ppermute | solution.py:17
  108.3 91.0 %copy-start.11 = (bf16[1,8,24,128]{3,2,1,0:T(8,128)(2,1)S(1)}, bf16[1,8,24,128]{3,2,1,0:T(8,128)(2,1)}, u32[]{:S(2)}) copy-start(bf16[1,8,24,128]{3,2,1,0:T(8,128)(2,1)} %copy-done.10) | copy-start | bytes 147460
  109.4 90.0 %copy-start.18 = (bf16[1,8,24,128]{3,2,1,0:T(8,128)(2,1)S(1)}, bf16[1,8,24,128]{3,2,1,0:T(8,128)(2,1)}, u32[]{:S(2)}) copy-start(bf16[1,8,24,128]{3,2,1,0:T(8,128)(2,1)} %get-tuple-element.103) | copy-start | bytes 147460
  109.4 90.0 %copy-start.17 = (bf16[1,8,24,128]{3,2,1,0:T(8,128)(2,1)S(1)}, bf16[1,8,24,128]{3,2,1,0:T(8,128)(2,1)}, u32[]{:S(2)}) copy-start(bf16[1,8,24,128]{3,2,1,0:T(8,128)(2,1)} %get-tuple-element.102) | copy-start | bytes 147460
  109.4 90.0 %copy-start.16 = (bf16[1,8,24,128]{3,2,1,0:T(8,128)(2,1)S(1)}, bf16[1,8,24,128]{3,2,1,0:T(8,128)(2,1)}, u32[]{:S(2)}) copy-start(bf16[1,8,24,128]{3,2,1,0:T(8,128)(2,1)} %get-tuple-element.101) | copy-start | bytes 147460
  109.4 90.2 %copy-start.9 = (bf16[1,8,24,128]{3,2,1,0:T(8,128)(2,1)S(1)}, bf16[1,8,24,128]{3,2,1,0:T(8,128)(2,1)}, u32[]{:S(2)}) copy-start(bf16[1,8,24,128]{3,2,1,0:T(8,128)(2,1)} %copy-done.8) | copy-start | bytes 147460
  152.8 41.1 %copy-start.20 = (f32[128]{0:T(128)}, f32[128]{0:T(128)S(1)}, u32[]{:S(2)}) copy-start(f32[128]{0:T(128)S(1)} %sub.99) | copy-start | bytes 1540
  189.4 62.3 %collective-permute-start.3 = (bf16[1,8,24,128]{3,2,1,0:T(8,128)(2,1)}, bf16[1,8,24,128]{3,2,1,0:T(8,128)(2,1)}, u32[]{:S(2)}, u32[]{:S(2)}) collective-permute-start(bf16[1,8,24,128]{3,2,1,0:T(8,128)(2,1)} %multiply_convert_fusion.2), channel_id=1, source_target_pairs={{0,64},{64,128},{128,192},{192,256},{256,320},{320,384},{384,448},... | collective-permute-start | bytes 147464 | tf_op jit(solution)/shard_map/ppermute | solution.py:17
  193.9 57.8 %collective-permute-start.2 = (bf16[1,8,24,128]{3,2,1,0:T(8,128)(2,1)}, bf16[1,8,24,128]{3,2,1,0:T(8,128)(2,1)}, u32[]{:S(2)}, u32[]{:S(2)}) collective-permute-start(bf16[1,8,24,128]{3,2,1,0:T(8,128)(2,1)} %multiply_convert_fusion.2), channel_id=1, source_target_pairs={{0,128},{64,192},{128,256},{192,320},{256,384},{320,448},{384,512}... | collective-permute-start | bytes 147464 | tf_op jit(solution)/shard_map/ppermute | solution.py:17
  237.8 10.1 %collective-permute-start.7 = (bf16[1,8,24,128]{2,1,3,0:T(8,128)(2,1)}, bf16[1,8,24,128]{2,1,3,0:T(8,128)(2,1)}, u32[]{:S(2)}, u32[]{:S(2)}) collective-permute-start(bf16[1,8,24,128]{2,1,3,0:T(8,128)(2,1)} %reshape.272), channel_id=1, source_target_pairs={{128,0},{192,64},{256,128},{320,192},{384,256},{448,320},{512,384}... | collective-permute-start | bytes 147464 | tf_op jit(solution)/shard_map/ppermute | solution.py:17
  239.1 9.9 %collective-permute-start.6 = (bf16[1,8,24,128]{2,1,3,0:T(8,128)(2,1)}, bf16[1,8,24,128]{2,1,3,0:T(8,128)(2,1)}, u32[]{:S(2)}, u32[]{:S(2)}) collective-permute-start(bf16[1,8,24,128]{2,1,3,0:T(8,128)(2,1)} %reshape.272), channel_id=1, source_target_pairs={{64,0},{128,64},{192,128},{256,192},{320,256},{384,320},{448,384},... | collective-permute-start | bytes 147464 | tf_op jit(solution)/shard_map/ppermute | solution.py:17
  258.2 134.3 %copy-start.19 = (bf16[1,8,24,128]{3,2,1,0:T(8,128)(2,1)S(1)}, bf16[1,8,24,128]{3,2,1,0:T(8,128)(2,1)}, u32[]{:S(2)}) copy-start(bf16[1,8,24,128]{3,2,1,0:T(8,128)(2,1)} %get-tuple-element.83) | copy-start | bytes 147460
  258.3 141.0 %copy-start.15 = (bf16[1,8,24,128]{3,2,1,0:T(8,128)(2,1)S(1)}, bf16[1,8,24,128]{3,2,1,0:T(8,128)(2,1)}, u32[]{:S(2)}) copy-start(bf16[1,8,24,128]{3,2,1,0:T(8,128)(2,1)} %get-tuple-element.74) | copy-start | bytes 147460
  258.3 141.0 %copy-start.14 = (bf16[1,8,24,128]{3,2,1,0:T(8,128)(2,1)S(1)}, bf16[1,8,24,128]{3,2,1,0:T(8,128)(2,1)}, u32[]{:S(2)}) copy-start(bf16[1,8,24,128]{3,2,1,0:T(8,128)(2,1)} %get-tuple-element.73) | copy-start | bytes 147460
  381.1 18.2 %copy-start.13 = (bf16[1,8,24,128]{3,2,1,0:T(8,128)(2,1)S(1)}, bf16[1,8,24,128]{3,2,1,0:T(8,128)(2,1)}, u32[]{:S(2)}) copy-start(bf16[1,8,24,128]{3,2,1,0:T(8,128)(2,1)} %get-tuple-element.72) | copy-start | bytes 147460
  381.1 18.2 %copy-start.12 = (bf16[1,8,24,128]{3,2,1,0:T(8,128)(2,1)S(1)}, bf16[1,8,24,128]{3,2,1,0:T(8,128)(2,1)}, u32[]{:S(2)}) copy-start(bf16[1,8,24,128]{3,2,1,0:T(8,128)(2,1)} %get-tuple-element.71) | copy-start | bytes 147460
  381.2 95.0 %collective-permute-start.19 = (bf16[64,128]{1,0:T(8,128)(2,1)S(1)}, bf16[64,128]{1,0:T(8,128)(2,1)S(1)}, u32[]{:S(2)}, u32[]{:S(2)}) collective-permute-start(bf16[64,128]{1,0:T(8,128)(2,1)S(1)} %convert.42), channel_id=1, source_target_pairs={{0,2},{1,3},{2,4},{3,5},{4,6},{5,7},{6,8},{7,9},{8,10},{9,11},{10,... | collective-permute-start | bytes 49160
  383.1 94.4 %collective-permute-start.20 = (bf16[64,128]{1,0:T(8,128)(2,1)S(1)}, bf16[64,128]{1,0:T(8,128)(2,1)S(1)}, u32[]{:S(2)}, u32[]{:S(2)}) collective-permute-start(bf16[64,128]{1,0:T(8,128)(2,1)S(1)} %convert.42), channel_id=1, source_target_pairs={{0,3},{1,4},{2,5},{3,6},{4,7},{5,8},{6,9},{7,10},{8,11},{9,12},{10... | collective-permute-start | bytes 49160
  384.4 99.2 %collective-permute-start.21 = (bf16[64,128]{1,0:T(8,128)(2,1)S(1)}, bf16[64,128]{1,0:T(8,128)(2,1)S(1)}, u32[]{:S(2)}, u32[]{:S(2)}) collective-permute-start(bf16[64,128]{1,0:T(8,128)(2,1)S(1)} %convert.42), channel_id=1, source_target_pairs={{0,4},{1,5},{2,6},{3,7},{4,8},{5,9},{6,10},{7,11},{8,12},{9,13},{1... | collective-permute-start | bytes 49160
  385.7 106.1 %collective-permute-start.22 = (bf16[64,128]{1,0:T(8,128)(2,1)S(1)}, bf16[64,128]{1,0:T(8,128)(2,1)S(1)}, u32[]{:S(2)}, u32[]{:S(2)}) collective-permute-start(bf16[64,128]{1,0:T(8,128)(2,1)S(1)} %convert.42), channel_id=1, source_target_pairs={{0,5},{1,6},{2,7},{3,8},{4,9},{5,10},{6,11},{7,12},{8,13},{9,14},{... | collective-permute-start | bytes 49160
  392.6 7.1 %copy-start.4 = (bf16[32,4,3456]{2,1,0:T(4,128)(2,1)S(1)}, bf16[32,4,3456]{2,1,0:T(4,128)(2,1)}, u32[]{:S(2)}) copy-start(bf16[32,4,3456]{2,1,0:T(4,128)(2,1)} %dot_general.35) | copy-start | bytes 2654212
  392.6 7.1 %copy-start.7 = (f32[192,32,4]{0,2,1:T(4,128)S(1)}, f32[192,32,4]{0,2,1:T(4,128)}, u32[]{:S(2)}) copy-start(f32[192,32,4]{0,2,1:T(4,128)} %reshape.281) | copy-start | bytes 294916
  392.6 7.1 %copy-start.31 = (f32[32]{0:T(128)S(1)}, f32[32]{0:T(128)}, u32[]{:S(2)}) copy-start(f32[32]{0:T(128)} %copy-done.30) | copy-start | bytes 388
  439.8 14.7 %copy-start.22 = (f32[128]{0:T(128)S(1)}, f32[128]{0:T(128)}, u32[]{:S(2)}) copy-start(f32[128]{0:T(128)} %copy-done.20) | copy-start | bytes 1540
  439.9 14.7 %copy-start.25 = (f32[128]{0:T(128)S(1)}, f32[128]{0:T(128)}, u32[]{:S(2)}) copy-start(f32[128]{0:T(128)} %copy-done.23) | copy-start | bytes 1540
  450.1 59.9 %copy-start.2 = (bf16[3456,128]{1,0:T(8,128)(2,1)S(1)}, bf16[3456,128]{1,0:T(8,128)(2,1)}, u32[]{:S(2)}) copy-start(bf16[3456,128]{1,0:T(8,128)(2,1)} %param.7) | copy-start | bytes 2654212
  456.5 9.3 %collective-permute-start.27 = (bf16[54,128]{1,0:T(8,128)(2,1)S(1)}, bf16[54,128]{1,0:T(8,128)(2,1)S(1)}, u32[]{:S(2)}, u32[]{:S(2)}) collective-permute-start(bf16[54,128]{1,0:T(8,128)(2,1)S(1)} %slice.505), channel_id=1, source_target_pairs={{0,10},{1,11},{2,12},{3,13},{4,14},{5,15},{6,16},{7,17},{8,18},{9,... | collective-permute-start | bytes 41480
  465.8 28.5 %collective-permute-start.23 = (bf16[64,128]{1,0:T(8,128)(2,1)S(1)}, bf16[64,128]{1,0:T(8,128)(2,1)S(1)}, u32[]{:S(2)}, u32[]{:S(2)}) collective-permute-start(bf16[64,128]{1,0:T(8,128)(2,1)S(1)} %convert.42), channel_id=1, source_target_pairs={{0,6},{1,7},{2,8},{3,9},{4,10},{5,11},{6,12},{7,13},{8,14},{9,15},... | collective-permute-start | bytes 49160
  476.2 22.1 %collective-permute-start.24 = (bf16[64,128]{1,0:T(8,128)(2,1)S(1)}, bf16[64,128]{1,0:T(8,128)(2,1)S(1)}, u32[]{:S(2)}, u32[]{:S(2)}) collective-permute-start(bf16[64,128]{1,0:T(8,128)(2,1)S(1)} %convert.42), channel_id=1, source_target_pairs={{0,7},{1,8},{2,9},{3,10},{4,11},{5,12},{6,13},{7,14},{8,15},{9,16}... | collective-permute-start | bytes 49160
  477.5 23.0 %collective-permute-start.25 = (bf16[64,128]{1,0:T(8,128)(2,1)S(1)}, bf16[64,128]{1,0:T(8,128)(2,1)S(1)}, u32[]{:S(2)}, u32[]{:S(2)}) collective-permute-start(bf16[64,128]{1,0:T(8,128)(2,1)S(1)} %convert.42), channel_id=1, source_target_pairs={{0,8},{1,9},{2,10},{3,11},{4,12},{5,13},{6,14},{7,15},{8,16},{9,17... | collective-permute-start | bytes 49160
  483.7 21.4 %collective-permute-start.26 = (bf16[64,128]{1,0:T(8,128)(2,1)S(1)}, bf16[64,128]{1,0:T(8,128)(2,1)S(1)}, u32[]{:S(2)}, u32[]{:S(2)}) collective-permute-start(bf16[64,128]{1,0:T(8,128)(2,1)S(1)} %convert.42), channel_id=1, source_target_pairs={{0,9},{1,10},{2,11},{3,12},{4,13},{5,14},{6,15},{7,16},{8,17},{9,1... | collective-permute-start | bytes 49160
  491.8 15.0 %collective-permute-start.18 = (bf16[64,128]{1,0:T(8,128)(2,1)S(1)}, bf16[64,128]{1,0:T(8,128)(2,1)S(1)}, u32[]{:S(2)}, u32[]{:S(2)}) collective-permute-start(bf16[64,128]{1,0:T(8,128)(2,1)S(1)} %convert.42), channel_id=1, source_target_pairs={{0,1},{1,2},{2,3},{3,4},{4,5},{5,6},{6,7},{7,8},{8,9},{9,10},{10,1... | collective-permute-start | bytes 49160
  494.4 23.3 %collective-permute-start.9 = (bf16[64,128]{1,0:T(8,128)(2,1)S(1)}, bf16[64,128]{1,0:T(8,128)(2,1)S(1)}, u32[]{:S(2)}, u32[]{:S(2)}) collective-permute-start(bf16[64,128]{1,0:T(8,128)(2,1)S(1)} %convert.43), channel_id=1, source_target_pairs={{0,2},{1,3},{2,4},{3,5},{4,6},{5,7},{6,8},{7,9},{8,10},{9,11},{10,... | collective-permute-start | bytes 49160
  498.3 22.9 %collective-permute-start.10 = (bf16[64,128]{1,0:T(8,128)(2,1)S(1)}, bf16[64,128]{1,0:T(8,128)(2,1)S(1)}, u32[]{:S(2)}, u32[]{:S(2)}) collective-permute-start(bf16[64,128]{1,0:T(8,128)(2,1)S(1)} %convert.43), channel_id=1, source_target_pairs={{0,3},{1,4},{2,5},{3,6},{4,7},{5,8},{6,9},{7,10},{8,11},{9,12},{10... | collective-permute-start | bytes 49160
  500.5 25.7 %collective-permute-start.11 = (bf16[64,128]{1,0:T(8,128)(2,1)S(1)}, bf16[64,128]{1,0:T(8,128)(2,1)S(1)}, u32[]{:S(2)}, u32[]{:S(2)}) collective-permute-start(bf16[64,128]{1,0:T(8,128)(2,1)S(1)} %convert.43), channel_id=1, source_target_pairs={{0,4},{1,5},{2,6},{3,7},{4,8},{5,9},{6,10},{7,11},{8,12},{9,13},{1... | collective-permute-start | bytes 49160
  505.1 22.9 %collective-permute-start.12 = (bf16[64,128]{1,0:T(8,128)(2,1)S(1)}, bf16[64,128]{1,0:T(8,128)(2,1)S(1)}, u32[]{:S(2)}, u32[]{:S(2)}) collective-permute-start(bf16[64,128]{1,0:T(8,128)(2,1)S(1)} %convert.43), channel_id=1, source_target_pairs={{0,5},{1,6},{2,7},{3,8},{4,9},{5,10},{6,11},{7,12},{8,13},{9,14},{... | collective-permute-start | bytes 49160
  506.8 8.3 %collective-permute-start.17 = (bf16[54,128]{1,0:T(8,128)(2,1)S(1)}, bf16[54,128]{1,0:T(8,128)(2,1)S(1)}, u32[]{:S(2)}, u32[]{:S(2)}) collective-permute-start(bf16[54,128]{1,0:T(8,128)(2,1)S(1)} %slice.504), channel_id=1, source_target_pairs={{0,10},{1,11},{2,12},{3,13},{4,14},{5,15},{6,16},{7,17},{8,18},{9,... | collective-permute-start | bytes 41480
  515.1 14.9 %collective-permute-start.13 = (bf16[64,128]{1,0:T(8,128)(2,1)S(1)}, bf16[64,128]{1,0:T(8,128)(2,1)S(1)}, u32[]{:S(2)}, u32[]{:S(2)}) collective-permute-start(bf16[64,128]{1,0:T(8,128)(2,1)S(1)} %convert.43), channel_id=1, source_target_pairs={{0,6},{1,7},{2,8},{3,9},{4,10},{5,11},{6,12},{7,13},{8,14},{9,15},... | collective-permute-start | bytes 49160
  517.7 12.3 %collective-permute-start.14 = (bf16[64,128]{1,0:T(8,128)(2,1)S(1)}, bf16[64,128]{1,0:T(8,128)(2,1)S(1)}, u32[]{:S(2)}, u32[]{:S(2)}) collective-permute-start(bf16[64,128]{1,0:T(8,128)(2,1)S(1)} %convert.43), channel_id=1, source_target_pairs={{0,7},{1,8},{2,9},{3,10},{4,11},{5,12},{6,13},{7,14},{8,15},{9,16}... | collective-permute-start | bytes 49160
  521.2 8.8 %collective-permute-start.15 = (bf16[64,128]{1,0:T(8,128)(2,1)S(1)}, bf16[64,128]{1,0:T(8,128)(2,1)S(1)}, u32[]{:S(2)}, u32[]{:S(2)}) collective-permute-start(bf16[64,128]{1,0:T(8,128)(2,1)S(1)} %convert.43), channel_id=1, source_target_pairs={{0,8},{1,9},{2,10},{3,11},{4,12},{5,13},{6,14},{7,15},{8,16},{9,17... | collective-permute-start | bytes 49160
  526.2 3.8 collective-permute-start.16
  528.0 5.1 collective-permute-start.8
  (14 other events, 30.9 us)
where the time goes:
time: 609 us; the launch traced here: 606 us
  blocking collectives  421 us (69%)
  starting transfers between devices  94.7 us (16%)
  local copies, waits for them, and re-layouts  62.9 us (10%)
  matrix products  8.45 us (1%)
  waiting for transfers between devices  7.69 us (1%)
  other arithmetic  7.58 us (1%)
    psum x6, blocking collectives, group_sums(): return lax.psum(totals, 'tm')  229 us
    unnamed x2, blocking collectives  192 us
    unnamed x20, starting transfers between devices  77.3 us
    unnamed x203, local copies, waits for them, and re-layouts  40.8 us
    ppermute x8, starting transfers between devices, from_behind(): return lax.ppermute(block, axis, route)  17.4 us
  transfers between devices with their start and end apart: 28, of which 3 were waited for; matrix products, arithmetic and copies ran while one was open for 10% of the time, Pallas kernels for 0%

commit v1 on v0

v1 whole, which is shorter than its diff:
```python
import math

import jax
import jax.numpy as jnp
from jax import lax
from jax.sharding import PartitionSpec as P

GROUPS = 32


EPSILON = 1e-06

FORWARD_DIMS = ("NDHWC", "DHWIO", "NDHWC")
TRANSPOSED_DIMS = ("NDHWC", "DHWOI", "NDHWC")
WEIGHT_DIMS = ("CDHWN", "IDHWO", "NDHWC")


def normalize(values):
    grouped = values.reshape(-1, GROUPS, values.shape[-1] // GROUPS)
    average = jnp.mean(grouped, axis=(0, 2))
    centered = grouped - average[None, :, None]
    variance = jnp.mean(centered * centered, axis=(0, 2))
    inv_scale = lax.rsqrt(variance + EPSILON)
    return (centered * inv_scale[None, :, None], inv_scale)


def norm_backward(grad_act, normed, inv_scale):
    logistic = jax.nn.sigmoid(normed)
    grad_normed = grad_act * logistic * (1.0 + normed * (1.0 - logistic))
    first_mean = jnp.mean(grad_normed, axis=(0, 2))
    second_mean = jnp.mean(grad_normed * normed, axis=(0, 2))
    return inv_scale[None, :, None] * (
        grad_normed - first_mean[None, :, None] - normed * second_mean[None, :, None]
    )


def kernel_of(weight):
    chans = weight.shape[1]
    return weight.reshape(3, 3, 3, weight.shape[0] // (27), chans)


def conv_clip(act, weight):
    out = lax.conv_general_dilated(
        act[None],
        kernel_of(weight),
        window_strides=(1, 1, 1),
        padding=((2, 0), (1, 1), (1, 1)),
        dimension_numbers=FORWARD_DIMS,
        preferred_element_type=jnp.float32,
    )
    return out[0]


def conv_window(window, weight):
    out = lax.conv_general_dilated(
        window[None],
        kernel_of(weight),
        window_strides=(1, 1, 1),
        padding=((0, 0), (1, 1), (1, 1)),
        dimension_numbers=FORWARD_DIMS,
        preferred_element_type=jnp.float32,
    )
    return out[0]


def conv_transposed(grad, weight):
    kernel = kernel_of(weight)[::-1, ::-1, ::-1]
    out = lax.conv_general_dilated(
        grad[None],
        kernel,
        window_strides=(1, 1, 1),
        padding=((0, 2), (1, 1), (1, 1)),
        dimension_numbers=TRANSPOSED_DIMS,
        preferred_element_type=jnp.float32,
    )
    return out[0]


def weight_grad(act, grad):
    padded = jnp.pad(act, ((2, 0), (1, 1), (1, 1), (0, 0)))
    out = lax.conv_general_dilated(
        padded[None],
        grad[None],
        window_strides=(1, 1, 1),
        padding="VALID",
        dimension_numbers=WEIGHT_DIMS,
        preferred_element_type=jnp.float32,
    )
    chans_in = act.shape[-1]
    return out.transpose(1, 2, 3, 0, 4).reshape(27 * chans_in, grad.shape[-1])


def body(video, cotangent, conv1_weight, conv2_weight):
    own_frame = video[0]
    grad_own = cotangent[0]
    layout = own_frame.shape
    height, width, chans = (layout[1], layout[2], layout[3])
    frames = lax.axis_size("tm")
    me = lax.axis_index("tm")
    cols = chans // frames
    grouping = (-1, GROUPS, chans // GROUPS)

    both = jnp.concatenate([own_frame, grad_own], axis=0)
    gathered = lax.all_gather(both, "tm", axis=0, tiled=False)
    clip = gathered[:, 0]
    grad_out = gathered[:, 1]
    clip_layout = clip.shape

    first_normed, first_scale = normalize(clip.astype(jnp.float32))
    first_act = (first_normed * jax.nn.sigmoid(first_normed)).astype(jnp.bfloat16).reshape(clip_layout)
    hidden = conv_clip(first_act, conv1_weight).astype(jnp.bfloat16)
    second_normed, second_scale = normalize(hidden.astype(jnp.float32))
    second_act = (
        (second_normed * jax.nn.sigmoid(second_normed)).astype(jnp.bfloat16).reshape(clip_layout)
    )
    second_padded = jnp.pad(second_act, ((2, 0), (0, 0), (0, 0), (0, 0)))
    window = lax.dynamic_slice_in_dim(second_padded, me, 3, axis=0)
    mixed = conv_window(window, conv2_weight)
    block_out = (own_frame.astype(jnp.float32) + mixed).astype(jnp.bfloat16)

    grad_second = conv_transposed(grad_out, conv2_weight)
    grad_hidden = norm_backward(grad_second.reshape(grouping), second_normed, second_scale)
    grad_hidden = grad_hidden.astype(jnp.bfloat16).reshape(clip_layout)
    grad_first = conv_transposed(grad_hidden, conv1_weight)
    grad_first_act = norm_backward(grad_first.reshape(grouping), first_normed, first_scale)
    grad_first_act = grad_first_act.reshape(clip_layout)
    grad_video = grad_own.astype(jnp.float32) + lax.dynamic_slice_in_dim(grad_first_act, me, 1, axis=0)

    my_cols = lambda values: lax.dynamic_slice_in_dim(values, me * cols, cols, axis=3)
    grad_w2 = weight_grad(second_act, my_cols(grad_out))
    grad_w1 = weight_grad(first_act, my_cols(grad_hidden))
    stacked = jnp.stack([grad_w1.reshape(-1), grad_w2.reshape(-1)])
    reduced = lax.psum_scatter(stacked, "dp", scatter_dimension=1, tiled=True)
    rows = grad_w1.shape[0] // lax.axis_size("dp")
    factor = 1.0 / math.sqrt(frames * lax.axis_size("dp") * height * width)
    total_w1 = reduced[0].reshape(rows, cols) * factor
    total_w2 = reduced[1].reshape(rows, cols) * factor
    return (block_out[None], grad_video[None], total_w1, total_w2)


def solution(mesh):
    placed = (P("dp", "tm", None, None, None), P("dp", "tm", None, None, None), P(), P())
    return jax.shard_map(
        body,
        mesh=mesh,
        in_specs=placed,
        out_specs=(
            P("dp", "tm", None, None, None),
            P("dp", "tm", None, None, None),
            P("dp", "tm"),
            P("dp", "tm"),
        ),
        check_vma=False,
    )
```

time: 609 us -> 474 us (0.78)
  the two profiles are of different devices: /device:TPU:32 before, /device:TPU:4 now
where the time goes in v1:
time: 474 us; the launch traced here: 465 us
  waiting for transfers between devices  323 us (68%)
  matrix products  73.3 us (15%)
  local copies, waits for them, and re-layouts  37.2 us (8%)
  other arithmetic  17 us (4%)
  between operations  14.8 us (3%)
    unnamed x3, waiting for transfers between devices  233 us
    all_gather x1, waiting for transfers between devices, body(): gathered = lax.all_gather(both, 'tm', axis=0, tiled=False)  90.2 us
    transpose x2, matrix products, weight_grad(): return out.transpose(1, 2, 3, 0, 4).reshape(27 * chans_in, grad.shape[-1])  47.1 us
    conv_general_dilated x2, matrix products, conv_transposed(): lax.conv_general_dilated(grad[None], kernel, window_strides=(1, 1, 1), pa...  18.1 us
    unnamed x48, local copies, waits for them, and re-layouts  14.1 us
  transfers between devices with their start and end apart: 2, of which 2 were waited for; matrix products, arithmetic and copies ran while one was open for 1% of the time, Pallas kernels for 0%

profile of v1, /device:TPU:4, one launch (start us, length us, event | category | flops | bytes accessed | tf_op | source)
XLA Modules:
  0.0 465.2 jit_solution(8605690357598905176)
XLA Ops:
  7.2 1.5 pad_maximum_fusion.1
  8.9 90.2 %all-gather.3.cloned.1.call-done = bf16[32,8,24,128]{3,2,1,0:T(8,128)(2,1)} async-done(((bf16[2,8,24,128]{3,2,1,0:T(8,128)(2,1)}), bf16[32,8,24,128]{3,2,1,0:T(8,128)(2,1)}) %all-gather.3.cloned.1.call-update) | async-done | bytes 1572880 | tf_op jit(solution)/shard_map/all_gather | solution.py:104
  99.1 1.7 convert_reduce_fusion
  100.7 2.7 fusion.122
  103.9 0.4 fusion.41
  104.7 0.5 fusion.84
  105.2 0.4 pad.14
  105.7 0.2 copy.101
  106.1 0.2 copy-done.13
  106.3 0.5 copy-done.18
  106.8 7.5 %fusion.26 = (f32[128]{0:T(128)S(1)}, bf16[16,8,8,4,128]{4,2,3,1,0:T(8,128)(2,1)S(1)}) fusion(pred[8,4]{0,1:T(4,128)(4,1)S(1)} %copy-done.13, bf16[3,3,3,128,128]{4,3,2,1,0:T(8,128)(2,1)S(1)} %bitcast.161, bf16[16,8,1,7,2,128]{5,3,4,1,0,2:T(8,128)(2,1)S(1)} %slice.26, bf16[16,8,1,8,4,128]{5,3,4,1,0,2:T(8,128)(2,1)S(1)} %copy.101), kind=kOutput, calls=%fused_computation.35 | convolution fusion | flops 3121610752 | bytes 3441184 | tf_op jit(solution)/shard_map/conv_general_dilated | solution.py:43
  114.8 1.4 copy.102
  116.2 0.6 fusion.25
  117.3 1.5 pad.18
  118.8 0.3 copy.110
  119.4 10.0 %fusion.23 = (f32[128]{0:T(128)S(1)}, f32[128]{0:T(128)S(1)}, f32[16,8,8,4,128]{4,2,3,1,0:T(8,128)}, f32[16,8,8,4,128]{4,2,3,1,0:T(8,128)}) fusion(bf16[16,8,8,4,128]{4,2,3,1,0:T(8,128)(2,1)S(1)} %get-tuple-element.40, f32[128]{0:T(128)S(1)} %mul.219, f32[128]{0:T(128)S(1)} %sub.135, pred[8,4]{0,1:T(4,128)(4,1)S(1)} %copy-done.13, ...), kind=kOutput, calls=%fused_computation.32 | convolution fusion | flops 3127902208 | bytes 7637024 | tf_op jit(solution)/shard_map/conv_general_dilated | solution.py:68
  129.8 0.6 dynamic-slice.2
  130.9 2.3 fusion.83
  133.4 8.1 %fusion.46 = f32[16,8,8,4,128]{4,2,3,1,0:T(8,128)S(1)} fusion(bf16[3,3,3,128,128]{4,3,2,1,0:T(8,128)(2,1)S(1)} %bitcast.162, bf16[16,8,1,7,1,128]{5,3,4,1,0,2:T(8,128)(2,1)S(1)} %get-tuple-element.32, bf16[16,8,1,7,1,128]{5,3,4,1,0,2:T(8,128)(2,1)S(1)} %get-tuple-element.31, bf16[16,8,1,8,4,128]{5,3,4,1,0,2:T(8,128)(2,1)S(1)} %fusion.83), kind=kOutput, calls=%fused_computation.57 | convolution fusion | flops 3122135040 | bytes 4489216 | tf_op jit(solution)/shard_map/conv_general_dilated | solution.py:68
  141.5 1.6 copy.111
  143.3 0.8 fusion.120
  144.2 1.4 copy.169
  145.6 2.9 multiply_convert_fusion
  148.6 1.1 copy-done.5
  149.7 1.2 dynamic-slice_bitcast_fusion
  151.2 0.6 sub.151
  152.1 0.6 mul.244
  152.7 3.2 copy.113
  156.1 0.3 copy.168
  156.4 0.5 pad_bitcast_fusion.1
  156.9 1.5 add_divide_fusion.1
  158.4 1.7 fusion.88
  160.1 23.4 %fusion.12 = f32[3,3,3,128,8]{4,3,2,1,0:T(8,128)S(1)} fusion(bf16[1,18,10,26,128]{4,3,2,1,0:T(8,128)(2,1)S(1)} %pad_bitcast_fusion.1, bf16[1,16,8,24,8]{4,3,2,1,0:T(8,128)(2,1)S(1)} %fusion.88), kind=kOutput, calls=%fused_computation.21 | convolution fusion | flops 169869312 | bytes 1357824 | tf_op jit(solution)/shard_map/transpose | solution.py:90
  183.6 1.5 stack_reshape_reshape.6
  185.1 0.5 pad_bitcast_fusion
  185.8 0.6 convolution_select_fusion
  186.4 0.7 copy.107
  187.1 23.6 %fusion.10 = f32[3,3,3,128,8]{4,3,2,1,0:T(8,128)S(1)} fusion(bf16[1,18,10,26,128]{4,3,2,1,0:T(8,128)(2,1)S(1)} %pad_bitcast_fusion, bf16[1,16,8,24,8]{4,3,2,1,0:T(8,128)(2,1)S(1)} %copy-done.6), kind=kOutput, calls=%fused_computation.19 | convolution fusion | flops 169869312 | bytes 1357824 | tf_op jit(solution)/shard_map/transpose | solution.py:90
  210.8 0.9 stack_reshape_reshape.7
  211.7 0.2 pad_maximum_fusion
  211.9 7.5 %copy.126 = f32[2,27648]{0,1:T(8,128)} copy(f32[2,27648]{1,0:T(2,128)S(1)} %pad_maximum_fusion) | data formatting | bytes 442368
  219.5 0.8 copy-done.8
  220.3 0.6 copy.123
  221.0 1.7 fusion.103
  222.7 232.5 %reduce-scatter.4.cloned.1.call-done = f32[432,2]{1,0:T(8,128)} async-done(((f32[27648,2]{1,0:T(8,128)}), f32[432,2]{1,0:T(8,128)}) %reduce-scatter.4.cloned.1.call-update) | async-done | bytes 3472
  455.2 1.2 fusion.124
  456.7 0.7 copy.125
  457.5 0.7 copy.124
  (96 shorter events, 4.8 us)
Async XLA Ops:
  7.2 112.3 %copy-start = (bf16[3456,128]{1,0:T(8,128)(2,1)S(1)}, bf16[3456,128]{1,0:T(8,128)(2,1)}, u32[]{:S(2)}) copy-start(bf16[3456,128]{1,0:T(8,128)(2,1)} %param.7) | copy-start | bytes 2654212
  7.2 91.9 %all-gather.3.cloned.1.call-start = ((), (), s32[]{:S(2)}) async-start(), calls=%async_computation.1 | async-start | bytes 1671168 | tf_op jit(solution)/shard_map/all_gather | solution.py:104
  8.8 446.4 %reduce-scatter.4.cloned.1.call-start = ((), (), s32[]{:S(2)}) async-start(), calls=%async_computation.2 | async-start | bytes 14376960
  99.1 4.8 %copy-start.2 = (bf16[32,8,24,128]{3,2,1,0:T(8,128)(2,1)S(1)}, bf16[32,8,24,128]{3,2,1,0:T(8,128)(2,1)}, u32[]{:S(2)}) copy-start(bf16[32,8,24,128]{3,2,1,0:T(8,128)(2,1)} %all-gather.3.cloned.1.call-done) | copy-start | bytes 4718596
  104.7 40.9 %copy-start.11 = (f32[128]{0:T(128)}, f32[128]{0:T(128)S(1)}, u32[]{:S(2)}) copy-start(f32[128]{0:T(128)S(1)} %mul.213) | copy-start | bytes 1540
  105.7 0.7 copy-start.13
  105.7 1.2 copy-start.18
  130.9 2.4 copy-start.19
  145.6 2.9 copy-start.4
  148.5 1.1 copy-start.5
  156.9 1.6 copy-start.17
  183.5 1.5 copy-start.3
  185.1 0.7 copy-start.14
  185.6 1.5 copy-start.6
  210.8 0.9 copy-start.7
  219.4 0.9 copy-start.8
  219.4 0.9 copy-start.10
  219.4 1.6 copy-start.9
  219.4 1.6 copy-start.12
  219.4 1.5 copy-start.15
  219.4 1.5 copy-start.16
  219.5 238.7 %copy-start.1 = (bf16[3456,128]{1,0:T(8,128)(2,1)S(1)}, bf16[3456,128]{1,0:T(8,128)(2,1)}, u32[]{:S(2)}) copy-start(bf16[3456,128]{1,0:T(8,128)(2,1)} %param.7) | copy-start | bytes 2654212
Sparse Core Ops, SparseCore 0:
  12.8 86.2 all-gather.2
  219.6 235.5 reduce-scatter.3
